TPU v7x, 256 devices: a whole 4x4x8 slice. The times are simulated.
256 devices in a mesh: heads: 32 (over z_hi, y, x), width: 8 (over z_lo, core).
Axes of the slice: x: 4, y: 4, z: 8 (z_hi: 2, z_lo: 4; z = z_hi * 4 + z_lo), core: 2. Of those that a mesh axis runs over, the one named last changes fastest.
Arguments:
- states: bfloat16 [1536, 6144], P('heads', 'width'), may hold values from -6 to 6
- segment_ids: int32 [1536], replicated, may hold values from 0 to 11, never falling along the last dimension, each value on 1 to 1344 neighbouring positions
- attn_gain: float32 [6144], P('width'), may hold values from 0.1 to 1.9
- attn_shift: float32 [6144], P('width'), may hold values from -3 to 3
- mlp_gain: float32 [6144], P('width'), may hold values from 0.1 to 1.9
- mlp_shift: float32 [6144], P('width'), may hold values from -3 to 3
- qkv_weight: bfloat16 [6144, 18432], P('width', 'heads'), may hold values from -0.078125 to 0.078125
- qkv_bias: float32 [18432], P('heads'), may hold values from -6 to 6
- dense_weight: bfloat16 [6144, 6144], P('heads', 'width'), may hold values from -0.078125 to 0.078125
- dense_bias: float32 [6144], P('width'), may hold values from -2 to 2
- up_weight: bfloat16 [6144, 24576], P('width', 'heads'), may hold values from -0.078125 to 0.078125
- up_bias: float32 [24576], P('heads'), may hold values from -3 to 3
- down_weight: bfloat16 [24576, 6144], P('heads', 'width'), may hold values from -0.0390625 to 0.0390625
- down_bias: float32 [6144], P('width'), may hold values from -2 to 2
Outputs:
- layer_out: bfloat16 [1536, 6144], P('heads', 'width')
- key_cache: bfloat16 [1536, 6144], P('width', 'heads')
- value_cache: bfloat16 [1536, 6144], P('width', 'heads')
Inputs may be any that keep to these rules, and one draw needn't show every extreme that they name: `segment_ids`: document numbers never fall along the tokens; each document has 1 to 1344 tokens and one has exactly 1344.
All inputs are finite; a program needn't handle non-finite values.
Results may differ from a plain program's by a relative error of at most 0.017.
Values may be sent and summed in bfloat16 or wider, within the bound.
No kernel may reach another device: no remote copies, remote signals or barrier semaphores. Data moves between devices by JAX's collectives and lax.ppermute only.
A program may use at most 64 MiB of HBM per device.

v0:
```python
import jax
import jax.numpy as jnp
from jax import lax
from jax.sharding import PartitionSpec as P

HD = 96
ROT = 24
D = 6144
norm_epsilon = 1e-05


def positions_of(segments):
    count = segments.shape[0]
    row_index = jnp.arange(count, dtype=jnp.int32)
    change = jnp.concatenate([jnp.ones((1,), bool), segments[1:] != segments[:-1]])
    first = lax.cummax(jnp.where(change, row_index, 0), axis=0)
    return (row_index - first).astype(jnp.float32)


def rotary(values, positions):
    half_rot = ROT // 2
    inverse = 10000.0 ** (-(jnp.arange(half_rot, dtype=jnp.float32) * 2.0 / ROT))
    angles = positions[:, None] * inverse[None, :]
    cosine = jnp.cos(angles)[:, None, :]
    sine_part = jnp.sin(angles)[:, None, :]
    first_half = values[..., :half_rot]
    second_half = values[..., half_rot:ROT]
    return jnp.concatenate(
        [
            first_half * cosine - second_half * sine_part,
            second_half * cosine + first_half * sine_part,
            values[..., ROT:],
        ],
        axis=-1,
    )


HEADS = ("hz", "hy", "hx")
WIDTH = ("wz", "wc")


def gather_heads(block):
    rows, cols = block.shape
    ny, nx = (lax.axis_size("hy"), lax.axis_size("hx"))
    spread = jnp.broadcast_to(block[None], (ny * nx,) + block.shape)
    block = lax.all_to_all(spread, ("hy", "hx"), 0, 0, tiled=False)
    nz = lax.axis_size("hz")
    block = block.reshape(ny, nx, nz, rows // nz, cols).transpose(2, 0, 1, 3, 4)
    return block.reshape(-1, cols)


def reduce_heads(partial):
    nz, ny, nx = [lax.axis_size(a) for a in HEADS]
    cols = partial.shape[1]
    rows = partial.shape[0] // (nz * ny * nx)
    part = partial.reshape(nz, ny * nx, rows, cols).transpose(1, 0, 2, 3)
    part = lax.all_to_all(part, ("hy", "hx"), 0, 0, tiled=False)
    total = jnp.sum(part.astype(jnp.float32), 0)
    part = lax.all_to_all(total.astype(jnp.bfloat16), "hz", 0, 0, tiled=False)
    return jnp.sum(part.astype(jnp.float32), 0)


def on_device(
    states,
    segment_ids,
    attn_gain,
    attn_shift,
    mlp_gain,
    mlp_shift,
    qkv_weight,
    qkv_bias,
    dense_weight,
    dense_bias,
    up_weight,
    up_bias,
    down_weight,
    down_bias,
):
    floats = states.astype(jnp.float32)
    nz = lax.axis_size("hz")
    z = lax.axis_index("hz")
    swaps = [
        lax.ppermute(states, "hz", [(i, (i + k) % nz) for i in range(nz)]) for k in range(1, nz)
    ]
    local = jnp.stack([jnp.sum(floats, -1), jnp.sum(floats * floats, -1)])
    group = nz * lax.axis_size(WIDTH)
    every = lax.all_to_all(
        jnp.broadcast_to(local[None], (group,) + local.shape), ("hz",) + WIDTH, 0, 0, tiled=False
    )
    stats = jnp.sum(every.reshape(nz, -1, 2, local.shape[1]), 1)
    pair = jnp.stack([states] + swaps)
    by_z = jnp.take(pair, (z - jnp.arange(nz)) % nz, axis=0).astype(jnp.float32)
    row_mean = (stats[:, 0] / D)[..., None]
    row_var = (stats[:, 1] / D)[..., None] - row_mean * row_mean
    normed = ((by_z - row_mean) * lax.rsqrt(row_var + norm_epsilon)).astype(jnp.bfloat16)
    qkv_cols = qkv_weight.shape[1]
    heads_dev = qkv_cols // (3 * HD)
    block_f = gather_heads(normed.reshape(-1, normed.shape[2])).astype(jnp.float32)
    attn_in = (block_f * attn_gain + attn_shift).astype(jnp.bfloat16)
    mlp_in = (block_f * mlp_gain + mlp_shift).astype(jnp.bfloat16)
    projected = jnp.concatenate(
        [
            jnp.dot(attn_in, qkv_weight, preferred_element_type=jnp.float32),
            jnp.dot(mlp_in, up_weight, preferred_element_type=jnp.float32),
        ],
        axis=1,
    )
    summed_proj = lax.psum(projected.astype(jnp.bfloat16), WIDTH)
    all_tokens = projected.shape[0]
    own_rows = all_tokens // lax.axis_size(WIDTH)
    row_zero = lax.axis_index(WIDTH) * own_rows
    positions = positions_of(segment_ids)
    own_segments = lax.dynamic_slice_in_dim(segment_ids, row_zero, own_rows)
    own_index = row_zero + jnp.arange(own_rows, dtype=jnp.int32)
    score_scale = 1.0 / HD**0.5
    own_positions = lax.dynamic_slice_in_dim(positions, row_zero, own_rows)
    shaped = (summed_proj[:, :qkv_cols].astype(jnp.float32) + qkv_bias).reshape(
        all_tokens, heads_dev, 3, HD
    )
    own_shaped = lax.dynamic_slice_in_dim(shaped, row_zero, own_rows)
    queries = rotary(own_shaped[:, :, 0, :], own_positions).astype(jnp.bfloat16)
    key_heads = rotary(shaped[:, :, 1, :], positions).astype(jnp.bfloat16)
    value_heads = shaped[:, :, 2, :].astype(jnp.bfloat16)
    width_cols = heads_dev * HD
    key_cache = lax.dynamic_slice_in_dim(key_heads, row_zero, own_rows).reshape(-1, width_cols)
    value_cache = lax.dynamic_slice_in_dim(value_heads, row_zero, own_rows).reshape(-1, width_cols)
    run_max = jnp.full((heads_dev, own_rows), -1e30, jnp.float32)
    count = all_tokens
    scores = (
        jnp.einsum("rhd,nhd->hrn", queries, key_heads, preferred_element_type=jnp.float32)
        * score_scale
    )
    key_index = jnp.arange(count, dtype=jnp.int32)
    allowed = (own_segments[:, None] == segment_ids[None, :]) & (
        key_index[None, :] <= own_index[:, None]
    )
    scores = jnp.where(allowed[None], scores, -1e30)
    new_max = jnp.maximum(run_max, jnp.max(scores, -1))
    weights = jnp.where(allowed[None], jnp.exp(scores - new_max[..., None]), 0.0)
    new_sum = jnp.sum(weights, -1)
    mixed = jnp.einsum(
        "hrn,nhd->hrd",
        weights.astype(jnp.bfloat16),
        value_heads,
        preferred_element_type=jnp.float32,
    )
    attended = (
        (mixed / new_sum[..., None])
        .transpose(1, 0, 2)
        .reshape(own_rows, heads_dev * HD)
        .astype(jnp.bfloat16)
    )
    attn_part = jnp.dot(
        lax.all_to_all(
            jnp.broadcast_to(attended[None], (lax.axis_size(WIDTH),) + attended.shape),
            WIDTH,
            0,
            0,
            tiled=False,
        ).reshape(-1, attended.shape[1]),
        dense_weight,
        preferred_element_type=jnp.float32,
    )
    hidden = jax.nn.gelu(
        summed_proj[:, qkv_cols:].astype(jnp.float32) + up_bias, approximate=False
    ).astype(jnp.bfloat16)
    hidden = lax.optimization_barrier(hidden)
    mlp_part = jnp.dot(hidden, down_weight, preferred_element_type=jnp.float32)
    summed = reduce_heads((attn_part + mlp_part).astype(jnp.bfloat16))
    layer_out = (floats + summed + dense_bias + down_bias).astype(jnp.bfloat16)
    return (layer_out, key_cache, value_cache)


def solution(mesh):
    devices = mesh.devices.reshape(2, 4, 4, 4, 2)
    fine = jax.sharding.Mesh(devices, HEADS + WIDTH)
    in_specs = (
        P(HEADS, WIDTH),
        P(),
        P(WIDTH),
        P(WIDTH),
        P(WIDTH),
        P(WIDTH),
        P(WIDTH, HEADS),
        P(HEADS),
        P(HEADS, WIDTH),
        P(WIDTH),
        P(WIDTH, HEADS),
        P(HEADS),
        P(HEADS, WIDTH),
        P(WIDTH),
    )
    out_specs = (P(HEADS, WIDTH), P(WIDTH, HEADS), P(WIDTH, HEADS))
    return jax.shard_map(
        on_device, mesh=fine, in_specs=in_specs, out_specs=out_specs, check_vma=False
    )
```

profile of v0, /device:TPU:2, one launch (start us, length us, event | category | flops | bytes accessed | tf_op | source)
XLA Modules:
  0.0 273.8 jit_solution(16590568960911276245)
XLA Ops:
  7.2 7.3 %collective-permute-start = (bf16[48,768]{1,0:T(8,128)(2,1)}, bf16[48,768]{1,0:T(8,128)(2,1)S(1)}, u32[]{:S(2)}, u32[]{:S(2)}) collective-permute-start(bf16[48,768]{1,0:T(8,128)(2,1)} %param.14), channel_id=1, source_target_pairs={{0,128},{128,0},{1,129},{129,1},{2,130},{130,2},{3,131},{131,3},{4... | collective-permute-start | bytes 221192 | tf_op jit(solution)/shard_map/ppermute | solution.py:83
  14.5 1.0 convert_reduce_fusion.1
  16.1 3.5 %all-to-all-start = ((f32[16,2,48]{2,1,0:T(2,128)}), f32[16,2,48]{2,1,0:T(2,128)S(1)}, u32[]{:S(2)}, u32[]{:S(2)}) async-start(f32[16,2,48]{2,1,0:T(2,128)} %broadcast_in_dim.49), calls=%async_computation | async-start | bytes 32768 | tf_op jit(solution)/shard_map/all_to_all | solution.py:87
  19.9 7.3 %all-to-all-done = f32[16,2,48]{2,1,0:T(2,128)S(1)} async-done(((f32[16,2,48]{2,1,0:T(2,128)}), f32[16,2,48]{2,1,0:T(2,128)S(1)}, u32[]{:S(2)}, u32[]{:S(2)}) %all-to-all-start) | async-done | bytes 6176 | tf_op jit(solution)/shard_map/all_to_all | solution.py:87
  27.4 0.9 pad_maximum_fusion.2
  29.2 37.4 %all_to_all.25 = bf16[16,96,768]{2,1,0:T(8,128)(2,1)S(1)} all-to-all(bf16[16,96,768]{2,1,0:T(8,128)(2,1)S(1)} %broadcast_in_dim.50), channel_id=1, replica_groups=mesh['hz'=2,'hy'=4,'hx'=4,'wz'=4,'wc'=2] {'hy','hx'}, dimensions={0} | all-to-all | bytes 4718592 | tf_op jit(solution)/shard_map/all_to_all | solution.py:46
  67.9 1.1 fusion.4
  69.1 1.6 convolution_convert_fusion.1
  70.7 2.1 convolution_convert_fusion
  72.8 2.2 pad_maximum_fusion
  77.3 99.5 %all-reduce.2.cloned.1.call-done = bf16[1536,1344]{0,1:T(8,128)(2,1)} async-done(((bf16[1536,1344]{0,1:T(8,128)(2,1)}), bf16[1536,1344]{0,1:T(8,128)(2,1)}) %all-reduce.2.cloned.1.call-update) | async-done | bytes 4128784 | tf_op jit(solution)/shard_map/psum | solution.py:108
  176.8 1.8 convert_add_fusion.1
  178.7 1.6 copy-done.1
  180.9 0.9 copy-done.2
  181.8 0.8 fusion.53
  182.6 0.7 fusion.18
  183.4 2.0 fusion.32
  185.4 1.0 broadcast_in_dim.93
  186.4 3.7 %all-to-all-start.2 = ((bf16[8,192,192]{2,1,0:T(8,128)(2,1)}), bf16[8,192,192]{2,1,0:T(8,128)(2,1)S(1)}, u32[]{:S(2)}, u32[]{:S(2)}) async-start(bf16[8,192,192]{2,1,0:T(8,128)(2,1)} %broadcast_in_dim.93), calls=%async_computation.2 | async-start | bytes 1572864 | tf_op jit(solution)/shard_map/all_to_all | solution.py:154
  190.2 12.2 %fusion.2 = bf16[1536,768]{0,1:T(8,128)(2,1)S(1)} fusion(bf16[1536,1344]{0,1:T(8,128)(2,1)} %all-reduce.2.cloned.1.call-done, f32[768]{0:T(1024)S(1)} %copy-done.12), kind=kLoop, calls=%fused_computation.4 | loop fusion | flops 79036416 | bytes 4721664 | tf_op jit(solution)/shard_map/convert_element_type | solution.py:166
  202.4 4.2 %fusion.55 = f32[1536,768]{1,0:T(8,128)} fusion(bf16[1536,768]{0,1:T(8,128)(2,1)S(1)} %fusion.2, bf16[768,768]{1,0:T(8,128)(2,1)S(1)} %copy-done.13), kind=kOutput, calls=%fused_computation.116 | convolution fusion | flops 1811939328 | bytes 8257536 | tf_op jit(solution)/shard_map/dot_general | solution.py:168
  206.6 4.3 %all-to-all-done.2 = bf16[8,192,192]{2,1,0:T(8,128)(2,1)S(1)} async-done(((bf16[8,192,192]{2,1,0:T(8,128)(2,1)}), bf16[8,192,192]{2,1,0:T(8,128)(2,1)S(1)}, u32[]{:S(2)}, u32[]{:S(2)}) %all-to-all-start.2) | async-done | bytes 589856 | tf_op jit(solution)/shard_map/all_to_all | solution.py:154
  210.9 3.1 %add_convert_fusion = bf16[1536,768]{1,0:T(8,128)(2,1)S(1)} fusion(f32[1536,768]{1,0:T(8,128)} %fusion.55, bf16[1536,192]{1,0:T(8,128)(2,1)S(1)} %bitcast.73, bf16[192,768]{1,0:T(8,128)(2,1)S(1)} %copy-done.3), kind=kOutput, calls=%fused_computation.12 | convolution fusion | flops 455344128 | bytes 7962624 | tf_op jit(solution)/shard_map/dot_general | solution.py:153
  214.2 36.6 %all_to_all.26 = bf16[16,2,48,768]{3,2,1,0:T(8,128)(2,1)S(1)} all-to-all(bf16[16,2,48,768]{3,2,1,0:T(8,128)(2,1)S(1)} %bitcast.67), channel_id=1, replica_groups=mesh['hz'=2,'hy'=4,'hx'=4,'wz'=4,'wc'=2] {'hy','hx'}, dimensions={0} | all-to-all | bytes 4718592 | tf_op jit(solution)/shard_map/all_to_all | solution.py:57
  250.9 1.0 reduce_sum.61
  251.9 5.0 %all-to-all-start.4 = ((bf16[2,48,768]{2,1,0:T(8,128)(2,1)}), bf16[2,48,768]{2,1,0:T(8,128)(2,1)S(1)}, u32[]{:S(2)}, u32[]{:S(2)}) async-start(bf16[2,48,768]{2,1,0:T(8,128)(2,1)} %reduce_sum.61), calls=%async_computation.4 | async-start | bytes 294912 | tf_op jit(solution)/shard_map/all_to_all | solution.py:59
  256.9 1.1 constant_dynamic-slice_fusion
  258.0 0.7 copy.80
  258.7 1.0 constant_dynamic-slice_fusion.1
  259.7 0.7 copy.79
  260.5 4.9 %all-to-all-done.4 = bf16[2,48,768]{2,1,0:T(8,128)(2,1)S(1)} async-done(((bf16[2,48,768]{2,1,0:T(8,128)(2,1)}), bf16[2,48,768]{2,1,0:T(8,128)(2,1)S(1)}, u32[]{:S(2)}, u32[]{:S(2)}) %all-to-all-start.4) | async-done | bytes 147488 | tf_op jit(solution)/shard_map/all_to_all | solution.py:59
  265.4 1.5 fusion.39
  (76 shorter events, 6.7 us)
Async XLA Ops:
  7.2 63.5 %copy-start = (bf16[768,768]{1,0:T(8,128)(2,1)S(1)}, bf16[768,768]{1,0:T(8,128)(2,1)}, u32[]{:S(2)}) copy-start(bf16[768,768]{1,0:T(8,128)(2,1)} %param.24) | copy-start | bytes 3538948
  7.2 20.2 %collective-permute-start = (bf16[48,768]{1,0:T(8,128)(2,1)}, bf16[48,768]{1,0:T(8,128)(2,1)S(1)}, u32[]{:S(2)}, u32[]{:S(2)}) collective-permute-start(bf16[48,768]{1,0:T(8,128)(2,1)} %param.14), channel_id=1, source_target_pairs={{0,128},{128,0},{1,129},{129,1},{2,130},{130,2},{3,131},{131,3},{4... | collective-permute-start | bytes 221192 | tf_op jit(solution)/shard_map/ppermute | solution.py:83
  16.1 11.1 %all-to-all-start = ((f32[16,2,48]{2,1,0:T(2,128)}), f32[16,2,48]{2,1,0:T(2,128)S(1)}, u32[]{:S(2)}, u32[]{:S(2)}) async-start(f32[16,2,48]{2,1,0:T(2,128)} %broadcast_in_dim.49), calls=%async_computation | async-start | bytes 32768 | tf_op jit(solution)/shard_map/all_to_all | solution.py:87
  19.6 157.1 %all-reduce.2.cloned.1.call-start = ((), (), s32[]{:S(2)}) async-start(), calls=%async_computation.5 | async-start | bytes 8257536 | tf_op jit(solution)/shard_map/psum | solution.py:108
  67.2 0.7 copy-start.5
  67.2 0.7 copy-start.6
  67.2 0.7 copy-start.7
  67.2 0.7 copy-start.8
  67.9 1.2 copy-start.14
  72.8 2.3 copy-start.4
  72.8 103.9 %copy-start.9 = (f32[576]{0:T(1024)S(1)}, f32[576]{0:T(1024)}, u32[]{:S(2)}) copy-start(f32[576]{0:T(1024)} %param.21) | copy-start | bytes 6916
  178.5 1.8 copy-start.1
  180.9 0.9 copy-start.2
  182.6 7.6 %copy-start.12 = (f32[768]{0:T(1024)S(1)}, f32[768]{0:T(1024)}, u32[]{:S(2)}) copy-start(f32[768]{0:T(1024)} %param.25) | copy-start | bytes 9220
  185.3 17.0 %copy-start.13 = (bf16[768,768]{1,0:T(8,128)(2,1)S(1)}, bf16[768,768]{1,0:T(8,128)(2,1)}, u32[]{:S(2)}) copy-start(bf16[768,768]{1,0:T(8,128)(2,1)} %param.26) | copy-start | bytes 3538948
  186.4 24.4 %all-to-all-start.2 = ((bf16[8,192,192]{2,1,0:T(8,128)(2,1)}), bf16[8,192,192]{2,1,0:T(8,128)(2,1)S(1)}, u32[]{:S(2)}, u32[]{:S(2)}) async-start(bf16[8,192,192]{2,1,0:T(8,128)(2,1)} %broadcast_in_dim.93), calls=%async_computation.2 | async-start | bytes 1572864 | tf_op jit(solution)/shard_map/all_to_all | solution.py:154
  202.3 8.5 %copy-start.3 = (bf16[192,768]{1,0:T(8,128)(2,1)S(1)}, bf16[192,768]{1,0:T(8,128)(2,1)}, u32[]{:S(2)}) copy-start(bf16[192,768]{1,0:T(8,128)(2,1)} %param.22) | copy-start | bytes 884740
  214.2 51.2 %copy-start.10 = (f32[768]{0:T(1024)S(1)}, f32[768]{0:T(1024)}, u32[]{:S(2)}) copy-start(f32[768]{0:T(1024)} %param.27) | copy-start | bytes 9220
  214.2 51.2 %copy-start.11 = (f32[768]{0:T(1024)S(1)}, f32[768]{0:T(1024)}, u32[]{:S(2)}) copy-start(f32[768]{0:T(1024)} %param.23) | copy-start | bytes 9220
  251.9 13.5 %all-to-all-start.4 = ((bf16[2,48,768]{2,1,0:T(8,128)(2,1)}), bf16[2,48,768]{2,1,0:T(8,128)(2,1)S(1)}, u32[]{:S(2)}, u32[]{:S(2)}) async-start(bf16[2,48,768]{2,1,0:T(8,128)(2,1)} %reduce_sum.61), calls=%async_computation.4 | async-start | bytes 294912 | tf_op jit(solution)/shard_map/all_to_all | solution.py:59
Sparse Core Ops, SparseCore 0:
  75.2 101.5 all-reduce.1
where the time goes:
time: 275 us; the launch traced here: 274 us
  waiting for transfers between devices  116 us (42%)
  blocking collectives  74 us (27%)
  other arithmetic  25.1 us (9%)
  starting transfers between devices  19.6 us (7%)
  between operations  14.4 us (5%)
  matrix products  13.7 us (5%)
  local copies, waits for them, and re-layouts  11 us (4%)
    psum x1, waiting for transfers between devices, on_device(): summed_proj = lax.psum(projected.astype(jnp.bfloat16), WIDTH)  99.5 us
    all_to_all x1, blocking collectives, gather_heads(): block = lax.all_to_all(spread, ('hy', 'hx'), 0, 0, tiled=False)  37.4 us
    all_to_all x1, blocking collectives, reduce_heads(): part = lax.all_to_all(part, ('hy', 'hx'), 0, 0, tiled=False)  36.6 us
    convert_element_type x1, other arithmetic, on_device(): hidden = jax.nn.gelu(summed_proj[:, qkv_cols:].astype(jnp.float32) + up_b...  12.2 us
    all_to_all x1, waiting for transfers between devices, on_device(): lax.all_to_all(jnp.broadcast_to(local[None], (group,) + local.shape), ('h...  7.28 us
    ppermute x1, starting transfers between devices, on_device(): lax.ppermute(states, 'hz', [(i, (i + k) % nz) for i in range(nz)])  7.28 us
  transfers between devices with their start and end apart: 5, of which 4 were waited for; matrix products, arithmetic and copies ran while one was open for 9% of the time, Pallas kernels for 0%

commit v1 on v0

--- a/solution.py
+++ b/solution.py
@@ -2,6 +2,7 @@
 import jax.numpy as jnp
 from jax import lax
 from jax.sharding import PartitionSpec as P
+from jax.lax import all_gather
 
 HD = 96
 ROT = 24
@@ -105,7 +106,7 @@
         ],
         axis=1,
     )
-    summed_proj = lax.psum(projected.astype(jnp.bfloat16), WIDTH)
+    summed_proj = jnp.sum(all_gather(projected.astype(jnp.bfloat16), WIDTH), 0)
     all_tokens = projected.shape[0]
     own_rows = all_tokens // lax.axis_size(WIDTH)
     row_zero = lax.axis_index(WIDTH) * own_rows

time: 275 us -> 510 us (1.85)
  waiting for transfers between devices: 116 us -> 361 us
  blocking collectives: 74 us -> 37.4 us
  other arithmetic: 25.1 us -> 39.1 us
  starting transfers between devices: 19.6 us -> 26.9 us
    all_gather x0 -> x1, waiting for transfers between devices: none -> 316 us  [on_device(): summed_proj = jnp.sum(all_gather(projected.astype(jnp.bfloat16), WIDTH), 0)]
    psum x1 -> x0, waiting for transfers between devices: 99.5 us -> none  [on_device(): summed_proj = lax.psum(projected.astype(jnp.bfloat16), WIDTH)]
    all_to_all x1 -> x0, blocking collectives: 36.6 us -> none  [reduce_heads(): part = lax.all_to_all(part, ('hy', 'hx'), 0, 0, tiled=False)]
    all_to_all x0 -> x1, waiting for transfers between devices: none -> 26.4 us  [reduce_heads(): part = lax.all_to_all(part, ('hy', 'hx'), 0, 0, tiled=False)]
    reduce_sum x0 -> x1, other arithmetic: none -> 14.1 us  [on_device(): summed_proj = jnp.sum(all_gather(projected.astype(jnp.bfloat16), WIDTH), 0)]
    all_to_all x0 -> x1, starting transfers between devices: none -> 7.41 us  [reduce_heads(): part = lax.all_to_all(part, ('hy', 'hx'), 0, 0, tiled=False)]
  transfers between devices with their start and end apart: 5 -> 6, of which waited for: 4 -> 5; matrix products, arithmetic and copies ran while one was open for 9% -> 5% of each run, Pallas kernels for 0% -> 0%
where the time goes in v1:
time: 510 us; the launch traced here: 505 us
  waiting for transfers between devices  361 us (71%)
  other arithmetic  39.1 us (8%)
  blocking collectives  37.4 us (7%)
  starting transfers between devices  26.9 us (5%)
  between operations  14.5 us (3%)
  matrix products  13.7 us (3%)
  local copies, waits for them, and re-layouts  13 us (3%)
    all_gather x1, waiting for transfers between devices, on_device(): summed_proj = jnp.sum(all_gather(projected.astype(jnp.bfloat16), WIDTH), 0)  316 us
    all_to_all x1, blocking collectives, gather_heads(): block = lax.all_to_all(spread, ('hy', 'hx'), 0, 0, tiled=False)  37.4 us
    all_to_all x1, waiting for transfers between devices, reduce_heads(): part = lax.all_to_all(part, ('hy', 'hx'), 0, 0, tiled=False)  26.4 us
    reduce_sum x1, other arithmetic, on_device(): summed_proj = jnp.sum(all_gather(projected.astype(jnp.bfloat16), WIDTH), 0)  14.1 us
    convert_element_type x1, other arithmetic, on_device(): hidden = jax.nn.gelu(summed_proj[:, qkv_cols:].astype(jnp.float32) + up_b...  12.2 us
  transfers between devices with their start and end apart: 6, of which 5 were waited for; matrix products, arithmetic and copies ran while one was open for 5% of the time, Pallas kernels for 0%

profile of v1, /device:TPU:2, one launch (start us, length us, event | category | flops | bytes accessed | tf_op | source)
XLA Modules:
  0.0 505.4 jit_solution(3123485457076879958)
XLA Ops:
  7.2 7.3 %collective-permute-start = (bf16[48,768]{1,0:T(8,128)(2,1)}, bf16[48,768]{1,0:T(8,128)(2,1)S(1)}, u32[]{:S(2)}, u32[]{:S(2)}) collective-permute-start(bf16[48,768]{1,0:T(8,128)(2,1)} %param.14), channel_id=1, source_target_pairs={{0,128},{128,0},{1,129},{129,1},{2,130},{130,2},{3,131},{131,3},{4... | collective-permute-start | bytes 221192 | tf_op jit(solution)/shard_map/ppermute | solution.py:84
  14.5 1.0 convert_reduce_fusion.1
  16.1 3.5 all-to-all-start
  19.9 7.3 %all-to-all-done = f32[16,2,48]{2,1,0:T(2,128)S(1)} async-done(((f32[16,2,48]{2,1,0:T(2,128)}), f32[16,2,48]{2,1,0:T(2,128)S(1)}, u32[]{:S(2)}, u32[]{:S(2)}) %all-to-all-start) | async-done | bytes 6176 | tf_op jit(solution)/shard_map/all_to_all | solution.py:88
  27.4 0.9 pad_maximum_fusion.2
  29.2 37.4 %all_to_all.25 = bf16[16,96,768]{2,1,0:T(8,128)(2,1)S(1)} all-to-all(bf16[16,96,768]{2,1,0:T(8,128)(2,1)S(1)} %broadcast_in_dim.50), channel_id=1, replica_groups=mesh['hz'=2,'hy'=4,'hx'=4,'wz'=4,'wc'=2] {'hy','hx'}, dimensions={0} | all-to-all | bytes 4718592 | tf_op jit(solution)/shard_map/all_to_all | solution.py:47
  67.9 1.1 fusion.4
  69.0 2.1 fusion.18
  71.1 1.6 fusion.19
  72.7 2.2 pad_maximum_fusion
  77.2 316.2 %all-gather.2.cloned.1.call-done = bf16[8,1536,1344]{1,2,0:T(8,128)(2,1)} async-done(((bf16[1,1536,1344]{1,2,0:T(8,128)(2,1)}), bf16[8,1536,1344]{1,2,0:T(8,128)(2,1)}) %all-gather.2.cloned.1.call-update) | async-done | bytes 33030160 | tf_op jit(solution)/shard_map/all_gather | solution.py:109
  393.4 14.1 %reduce_sum.72 = bf16[1536,1344]{0,1:T(8,128)(2,1)} reduce(bf16[8,1536,1344]{1,2,0:T(8,128)(2,1)} %all-gather.2.cloned.1.call-done, bf16[]{:T(256)} %constant.34.clone.1), dimensions={0}, to_apply=%region_3.4 | reduce | flops 14450688 | bytes 37158912 | tf_op jit(solution)/shard_map/reduce_sum | solution.py:109
  407.4 1.8 convert_add_fusion.1
  409.3 1.7 copy-done.2
  411.6 0.8 fusion.55
  413.2 2.0 fusion.34
  415.3 1.0 broadcast_in_dim.93
  416.3 3.7 all-to-all-start.2
  420.0 12.2 %fusion.2 = bf16[1536,768]{0,1:T(8,128)(2,1)S(1)} fusion(bf16[1536,1344]{0,1:T(8,128)(2,1)} %reduce_sum.72, f32[768]{0:T(1024)S(1)} %copy-done.13), kind=kLoop, calls=%fused_computation.4 | loop fusion | flops 79036416 | bytes 4721664 | tf_op jit(solution)/shard_map/convert_element_type | solution.py:167
  432.2 4.2 fusion.57
  436.4 4.3 all-to-all-done.2
  440.7 3.1 add_convert_fusion
  443.8 1.6 copy.98
  445.5 7.4 %all-to-all-start.3 = ((bf16[16,2,48,768]{3,2,1,0:T(8,128)(2,1)}), bf16[16,2,48,768]{3,2,1,0:T(8,128)(2,1)S(1)}, u32[]{:S(2)}, u32[]{:S(2)}) async-start(bf16[16,2,48,768]{3,2,1,0:T(8,128)(2,1)} %bitcast.71), calls=%async_computation.3 | async-start | bytes 4718592 | tf_op jit(solution)/shard_map/all_to_all | solution.py:58
  452.9 1.6 constant_dynamic-slice_fusion.1
  454.5 1.6 copy.77
  456.2 26.4 %all-to-all-done.3 = bf16[16,2,48,768]{3,2,1,0:T(8,128)(2,1)S(1)} async-done(((bf16[16,2,48,768]{3,2,1,0:T(8,128)(2,1)}), bf16[16,2,48,768]{3,2,1,0:T(8,128)(2,1)S(1)}, u32[]{:S(2)}, u32[]{:S(2)}) %all-to-all-start.3) | async-done | bytes 2359328 | tf_op jit(solution)/shard_map/all_to_all | solution.py:58
  482.6 1.0 reduce_sum.74
  483.6 4.9 all-to-all-start.4
  488.5 1.1 constant_dynamic-slice_fusion
  490.3 6.7 %all-to-all-done.4 = bf16[2,48,768]{2,1,0:T(8,128)(2,1)S(1)} async-done(((bf16[2,48,768]{2,1,0:T(8,128)(2,1)}), bf16[2,48,768]{2,1,0:T(8,128)(2,1)S(1)}, u32[]{:S(2)}, u32[]{:S(2)}) %all-to-all-start.4) | async-done | bytes 147488 | tf_op jit(solution)/shard_map/all_to_all | solution.py:60
  497.0 1.5 fusion.41
  (80 shorter events, 7.8 us)
Async XLA Ops:
  7.2 61.8 %copy-start = (bf16[768,768]{1,0:T(8,128)(2,1)S(1)}, bf16[768,768]{1,0:T(8,128)(2,1)}, u32[]{:S(2)}) copy-start(bf16[768,768]{1,0:T(8,128)(2,1)} %param.24) | copy-start | bytes 3538948
  7.2 20.2 %collective-permute-start = (bf16[48,768]{1,0:T(8,128)(2,1)}, bf16[48,768]{1,0:T(8,128)(2,1)S(1)}, u32[]{:S(2)}, u32[]{:S(2)}) collective-permute-start(bf16[48,768]{1,0:T(8,128)(2,1)} %param.14), channel_id=1, source_target_pairs={{0,128},{128,0},{1,129},{129,1},{2,130},{130,2},{3,131},{131,3},{4... | collective-permute-start | bytes 221192 | tf_op jit(solution)/shard_map/ppermute | solution.py:84
  16.1 11.1 %all-to-all-start = ((f32[16,2,48]{2,1,0:T(2,128)}), f32[16,2,48]{2,1,0:T(2,128)S(1)}, u32[]{:S(2)}, u32[]{:S(2)}) async-start(f32[16,2,48]{2,1,0:T(2,128)} %broadcast_in_dim.49), calls=%async_computation | async-start | bytes 32768 | tf_op jit(solution)/shard_map/all_to_all | solution.py:88
  19.6 373.7 %all-gather.2.cloned.1.call-start = ((), (), s32[]{:S(2)}) async-start(), calls=%async_computation.5 | async-start | bytes 37158912 | tf_op jit(solution)/shard_map/all_gather | solution.py:109
  67.2 0.7 copy-start.6
  67.2 0.7 copy-start.7
  67.2 0.7 copy-start.8
  67.2 0.7 copy-start.9
  69.0 2.1 copy-start.15
  72.7 2.2 copy-start.5
  77.2 330.3 %copy-start.10 = (f32[576]{0:T(1024)S(1)}, f32[576]{0:T(1024)}, u32[]{:S(2)}) copy-start(f32[576]{0:T(1024)} %param.21) | copy-start | bytes 6916
  409.2 1.8 copy-start.2
  411.6 3.5 copy-start.3
  412.5 7.6 %copy-start.13 = (f32[768]{0:T(1024)S(1)}, f32[768]{0:T(1024)}, u32[]{:S(2)}) copy-start(f32[768]{0:T(1024)} %param.25) | copy-start | bytes 9220
  415.2 17.0 %copy-start.14 = (bf16[768,768]{1,0:T(8,128)(2,1)S(1)}, bf16[768,768]{1,0:T(8,128)(2,1)}, u32[]{:S(2)}) copy-start(bf16[768,768]{1,0:T(8,128)(2,1)} %param.26) | copy-start | bytes 3538948
  416.3 24.4 %all-to-all-start.2 = ((bf16[8,192,192]{2,1,0:T(8,128)(2,1)}), bf16[8,192,192]{2,1,0:T(8,128)(2,1)S(1)}, u32[]{:S(2)}, u32[]{:S(2)}) async-start(bf16[8,192,192]{2,1,0:T(8,128)(2,1)} %broadcast_in_dim.93), calls=%async_computation.2 | async-start | bytes 1572864 | tf_op jit(solution)/shard_map/all_to_all | solution.py:155
  432.2 8.5 %copy-start.4 = (bf16[192,768]{1,0:T(8,128)(2,1)S(1)}, bf16[192,768]{1,0:T(8,128)(2,1)}, u32[]{:S(2)}) copy-start(bf16[192,768]{1,0:T(8,128)(2,1)} %param.22) | copy-start | bytes 884740
  443.8 54.7 %copy-start.1 = (bf16[768,768]{1,0:T(8,128)(2,1)S(1)}, bf16[768,768]{1,0:T(8,128)(2,1)}, u32[]{:S(2)}) copy-start(bf16[768,768]{1,0:T(8,128)(2,1)} %param.24) | copy-start | bytes 3538948
  445.5 51.5 %copy-start.11 = (f32[768]{0:T(1024)S(1)}, f32[768]{0:T(1024)}, u32[]{:S(2)}) copy-start(f32[768]{0:T(1024)} %param.27) | copy-start | bytes 9220
  445.5 51.5 %copy-start.12 = (f32[768]{0:T(1024)S(1)}, f32[768]{0:T(1024)}, u32[]{:S(2)}) copy-start(f32[768]{0:T(1024)} %param.23) | copy-start | bytes 9220
  445.5 37.1 %all-to-all-start.3 = ((bf16[16,2,48,768]{3,2,1,0:T(8,128)(2,1)}), bf16[16,2,48,768]{3,2,1,0:T(8,128)(2,1)S(1)}, u32[]{:S(2)}, u32[]{:S(2)}) async-start(bf16[16,2,48,768]{3,2,1,0:T(8,128)(2,1)} %bitcast.71), calls=%async_computation.3 | async-start | bytes 4718592 | tf_op jit(solution)/shard_map/all_to_all | solution.py:58
  483.6 13.4 %all-to-all-start.4 = ((bf16[2,48,768]{2,1,0:T(8,128)(2,1)}), bf16[2,48,768]{2,1,0:T(8,128)(2,1)S(1)}, u32[]{:S(2)}, u32[]{:S(2)}) async-start(bf16[2,48,768]{2,1,0:T(8,128)(2,1)} %reduce_sum.74), calls=%async_computation.4 | async-start | bytes 294912 | tf_op jit(solution)/shard_map/all_to_all | solution.py:60
Sparse Core Ops, SparseCore 0:
  75.1 318.2 all-gather.1
